TPU v7x, 32 devices: a whole 2x2x4 slice. The times are simulated.
32 devices in a mesh: req: 8 (over y, x, core), tp: 4 (over z).
Axes of the slice: x: 2, y: 2, z: 4, core: 2. Of those that a mesh axis runs over, the one named last changes fastest.
Arguments:
- queries: bfloat16 [1536, 2560], P('req', 'tp'), may hold values from -5 to 5
- new_keys: bfloat16 [1536, 512], P('req', 'tp'), may hold values from -5 to 5
- new_values: bfloat16 [1536, 512], P('req', 'tp'), may hold values from -5 to 5
- key_pages: bfloat16 [512, 64, 512], P('req', None, 'tp'), may hold values from -5 to 5
- value_pages: bfloat16 [512, 64, 512], P('req', None, 'tp'), may hold values from -5 to 5
- page_table: int32 [32, 16], P('req'), may hold values from 0 to 511, as said below
- cache_lengths: int32 [32], P('req'), may hold values from 2 to 1024, as said below
- parents: int32 [32, 48], P('req'), may hold values from -1 to 46, as said below
- residual: bfloat16 [1536, 2560], P('req'), may hold values from -6 to 6
- out_weight: bfloat16 [2560, 2560], P('tp'), may hold values from -0.125 to 0.125
- norm_gain: float32 [2560], replicated, may hold values from 0.1 to 1.9
- router_weight: float32 [2560, 16], replicated, may hold values from -0.125 to 0.125
- routes: int32 [1536, 6], P('req'), may hold values from 0 to 15, all different within a row; in each aligned block of 192 rows (0 to 191, 192 to 383, ...) at most 91 rows name the same one
- expert_gate_up: bfloat16 [16, 2560, 2, 1536], P('req', None, None, 'tp'), may hold values from -0.125 to 0.125
- expert_down: bfloat16 [16, 1536, 2560], P('req', 'tp'), may hold values from -0.15625 to 0.15625
- shared_gate_up: bfloat16 [2560, 2, 1536], P(None, None, 'tp'), may hold values from -0.125 to 0.125
- shared_down: bfloat16 [1536, 2560], P('tp'), may hold values from -0.15625 to 0.15625
Outputs:
- layer_out: bfloat16 [1536, 2560], P('req', 'tp')
Inputs may be any that keep to these rules, and one draw needn't show every extreme that they name: `page_table`: the pages of the 4 requests of the d-th block of 4 rows are the d-th block of 64 pages of the pool, each named once. `cache_lengths`: some request holds 1024 positions. parents[r, 0] = -1, and 0 <= parents[r, i] < i for i >= 1. `routes`: A token's 6 experts differ. In each aligned block of 192 rows no expert is named by more than 91 rows, and in some block one expert is named by exactly 91.
All inputs are finite; a program needn't handle non-finite values.
Results may differ from a plain program's by a relative error of at most 0.02.
Values may be sent and summed in bfloat16 or wider, within the bound.
No kernel may reach another device: no remote copies, remote signals or barrier semaphores. Data moves between devices by JAX's collectives and lax.ppermute only.
A program may use at most 128 MiB of HBM per device.

v0:
```python
import math
import jax
import jax.numpy as jnp
from jax import lax
from jax.sharding import PartitionSpec as P

QH = 20
KVH = 4
HD = 128
EPSILON = 1e-06
NEGATIVE = -1e30


def rounded(values):
    return lax.optimization_barrier(values.astype(jnp.bfloat16)).astype(jnp.float32)


def ancestors(parents):
    tree_size = parents.shape[-1]
    position = jnp.arange(tree_size, dtype=jnp.int32)
    adjacency = (parents[..., :, None] == position[None, :]) | (
        position[:, None] == position[None, :]
    )
    closure = adjacency.astype(jnp.float32)
    for doubling in range(max(1, (tree_size - 1).bit_length())):
        closure = jnp.minimum(
            jnp.einsum("...ij,...jk->...ik", closure, closure, precision=lax.Precision.HIGHEST), 1.0
        )
    return closure > 0.5


def tree_attention(queries, cache_keys, cache_values, new_keys, new_values, lengths, allowed):
    scaling = 1.0 / math.sqrt(queries.shape[-1])
    cache_scores = (
        jnp.einsum("rtkgd,rckd->rkgtc", queries, cache_keys, preferred_element_type=jnp.float32)
        * scaling
    )
    tree_scores = (
        jnp.einsum("rtkgd,rskd->rkgts", queries, new_keys, preferred_element_type=jnp.float32)
        * scaling
    )
    live = jnp.arange(cache_keys.shape[1], dtype=jnp.int32)[None, :] < lengths[:, None]
    cache_scores = jnp.where(live[:, None, None, None, :], cache_scores, NEGATIVE)
    tree_scores = jnp.where(allowed[:, None, None, :, :], tree_scores, NEGATIVE)
    highest = jnp.maximum(jnp.max(cache_scores, axis=-1), jnp.max(tree_scores, axis=-1))[..., None]
    cache_exp = jnp.exp(cache_scores - highest)
    tree_exp = jnp.exp(tree_scores - highest)
    denominator = (jnp.sum(cache_exp, axis=-1) + jnp.sum(tree_exp, axis=-1))[..., None]
    cache_probs = (cache_exp / denominator).astype(jnp.bfloat16)
    tree_probs = (tree_exp / denominator).astype(jnp.bfloat16)
    mixed = jnp.einsum(
        "rkgtc,rckd->rtkgd", cache_probs, cache_values, preferred_element_type=jnp.float32
    )
    mixed = mixed + jnp.einsum(
        "rkgts,rskd->rtkgd", tree_probs, new_values, preferred_element_type=jnp.float32
    )
    return mixed.astype(jnp.bfloat16).reshape(queries.shape[0], queries.shape[1], -1)


def place_rows(routes, experts_local, groups, capacity):
    flat_expert = routes.reshape(-1)
    expert_ids = jnp.arange(experts_local * groups, dtype=jnp.int32)
    onehot = (flat_expert[:, None] == expert_ids[None, :]).astype(jnp.int32)
    earlier = jnp.cumsum(onehot, axis=0) - onehot
    rank = jnp.sum(earlier * onehot, axis=1)
    owner = flat_expert // experts_local
    local_expert = flat_expert % experts_local
    return (local_expert * groups + owner) * capacity + rank


def fill_outbox(row_values, slot_index, top_count, lead_shape):
    repeated = jnp.repeat(row_values, top_count, axis=0)
    outbox = jnp.zeros(
        (lead_shape[0] * lead_shape[1] * lead_shape[2], row_values.shape[1]), row_values.dtype
    )
    outbox = outbox.at[slot_index].set(repeated)
    return outbox.reshape(lead_shape + (row_values.shape[1],))


def shards(
    queries,
    new_keys,
    new_values,
    key_pages,
    value_pages,
    page_table,
    cache_lengths,
    parents,
    residual,
    out_weight,
    norm_gain,
    router_weight,
    routes,
    expert_gate_up,
    expert_down,
    shared_gate_up,
    shared_down,
):
    groups = lax.axis_size("req")
    tp_count = lax.axis_size("tp")
    requests = parents.shape[0]
    tree_size = parents.shape[1]
    row_count = requests * tree_size
    kv_local = new_keys.shape[1] // HD
    head_ratio = QH // KVH
    model_width = residual.shape[1]
    part_width = model_width // tp_count
    pages_dev = key_pages.shape[0]
    local_pages = page_table - lax.axis_index("req") * pages_dev
    cache_keys = key_pages[local_pages].reshape(requests, -1, kv_local, HD)
    cache_values = value_pages[local_pages].reshape(requests, -1, kv_local, HD)
    head_outputs = tree_attention(
        queries.reshape(requests, tree_size, kv_local, head_ratio, HD),
        cache_keys,
        cache_values,
        new_keys.reshape(requests, tree_size, kv_local, HD),
        new_values.reshape(requests, tree_size, kv_local, HD),
        cache_lengths,
        ancestors(parents),
    )
    attn_terms = jnp.dot(
        head_outputs.reshape(row_count, -1), out_weight, preferred_element_type=jnp.float32
    )
    column = lax.axis_index("tp") * part_width
    experts_local = expert_gate_up.shape[0]
    top_count = routes.shape[1]
    expert_count = experts_local * groups
    capacity = max(10 * requests, row_count * top_count * 5 // (4 * expert_count) + 1)
    slot_index = place_rows(routes, experts_local, groups, capacity)
    lead_shape = (experts_local, groups, capacity)
    attn_out = lax.psum(attn_terms.astype(jnp.bfloat16), "tp").astype(jnp.float32)
    hidden = rounded(residual.astype(jnp.float32) + attn_out)
    rstd = lax.rsqrt(jnp.mean(hidden * hidden, axis=1, keepdims=True) + EPSILON)
    normed = hidden * rstd * norm_gain
    logits = jnp.dot(normed, router_weight, precision=lax.Precision.HIGHEST)
    normed_bf = normed.astype(jnp.bfloat16)
    hidden_part = lax.dynamic_slice_in_dim(hidden, column, part_width, 1)
    outbox = fill_outbox(normed_bf, slot_index, top_count, lead_shape)
    arrived = lax.all_to_all(outbox, "req", split_axis=1, concat_axis=1, tiled=True)
    arrived = arrived.reshape(experts_local, groups * capacity, model_width)
    gate_up = jnp.einsum(
        "emd,edcf->emcf", arrived, expert_gate_up, preferred_element_type=jnp.float32
    )
    act = (jax.nn.silu(gate_up[:, :, 0]) * gate_up[:, :, 1]).astype(jnp.bfloat16)
    partial_value = rounded(
        jnp.einsum("emf,efd->emd", act, expert_down, preferred_element_type=jnp.float32)
    )
    summed = lax.psum_scatter(
        partial_value.astype(jnp.bfloat16), "tp", scatter_dimension=2, tiled=True
    )
    outputs = summed.reshape(experts_local, groups, capacity, part_width)
    returned = lax.all_to_all(outputs, "req", split_axis=1, concat_axis=1, tiled=True).reshape(
        -1, part_width
    )
    picked = returned[slot_index].astype(jnp.float32).reshape(row_count, top_count, part_width)
    expert_ids = jnp.arange(expert_count, dtype=jnp.int32)
    chosen = jnp.sum(
        jnp.where(routes[:, :, None] == expert_ids[None, None, :], logits[:, None, :], 0.0), axis=-1
    )
    gate_values = jax.nn.sigmoid(chosen)
    gate_values = gate_values / jnp.sum(gate_values, axis=1, keepdims=True)
    routed = jnp.sum(picked * gate_values[:, :, None], axis=1)
    shared_gu = jnp.einsum(
        "td,dcf->tcf", normed_bf, shared_gate_up, preferred_element_type=jnp.float32
    )
    shared_act = (jax.nn.silu(shared_gu[:, 0]) * shared_gu[:, 1]).astype(jnp.bfloat16)
    shared_terms = jnp.dot(shared_act, shared_down, preferred_element_type=jnp.float32)
    shared_out = lax.psum_scatter(
        shared_terms.astype(jnp.bfloat16), "tp", scatter_dimension=1, tiled=True
    ).astype(jnp.float32)
    return (hidden_part + shared_out + routed).astype(jnp.bfloat16)


def solution(mesh):
    in_specs = (
        P("req", "tp"),
        P("req", "tp"),
        P("req", "tp"),
        P("req", None, "tp"),
        P("req", None, "tp"),
        P("req", None),
        P("req"),
        P("req", None),
        P("req", None),
        P("tp", None),
        P(),
        P(),
        P("req", None),
        P("req", None, None, "tp"),
        P("req", "tp", None),
        P(None, None, "tp"),
        P("tp", None),
    )
    out_specs = P("req", "tp")
    return jax.shard_map(shards, mesh=mesh, in_specs=in_specs, out_specs=out_specs, check_vma=False)
```

profile of v0, /device:TPU:0, one launch (start us, length us, event | category | flops | bytes accessed | tf_op | source)
XLA Modules:
  0.0 486.2 jit_solution(5703992235077245131)
XLA Ops:
  6.6 0.8 compare_select_fusion.4
  7.5 0.8 iota_compare_fusion.5
  8.3 2.0 reshape.306
  10.2 1.0 convolution_minimum_fusion.5
  11.2 0.2 convolution_minimum_fusion.4
  11.5 0.2 convolution_minimum_fusion.3
  11.7 0.2 convolution_minimum_fusion.2
  11.9 0.2 convolution_minimum_fusion.1
  12.2 0.2 fusion.22
  12.4 0.1 copy.58
  12.5 2.9 gather_fusion.1
  15.4 2.1 bitcast_reduce_fusion
  17.6 0.4 fusion.55
  18.0 1.4 copy-done.2
  19.4 1.0 fusion.8
  20.4 0.1 fusion.28
  20.5 2.9 gather_fusion
  23.4 3.5 fusion.11
  26.9 0.3 fusion.21
  27.2 0.1 copy.61
  27.4 1.9 convolution_convert_fusion.2
  29.3 0.2 reduce-scatter.9.cloned.1.call-start
  29.6 0.1 copy.63
  29.7 0.1 eq.80
  29.8 0.1 eq.76
  30.0 0.1 reshape.311
  30.1 4.5 reduce-window.6
  34.7 0.4 slice_reduce_fusion
  35.1 0.2 reduce-window.9
  35.3 0.1 broadcast_add_fusion
  35.5 46.5 %all-reduce.2.cloned.1.call-done = bf16[192,2560]{1,0:T(8,128)(2,1)} async-done(((bf16[192,2560]{1,0:T(8,128)(2,1)}), bf16[192,2560]{1,0:T(8,128)(2,1)}) %all-reduce.2.cloned.1.call-update) | async-done | bytes 983056 | tf_op jit(solution)/shard_map/psum | solution.py:131
  82.0 1.7 add_convert_fusion
  83.7 0.3 multiply_reduce_fusion.1
  84.0 0.3 fusion.15
  84.3 4.0 broadcast_in_dim.72
  88.3 10.2 %reshape.347 = bf16[1152,2560]{1,0:T(8,128)(2,1)} reshape(bf16[192,6,2560]{2,1,0:T(8,128)(2,1)} %broadcast_in_dim.72) | data formatting | bytes 11796480 | tf_op jit(solution)/shard_map/reshape | solution.py:72
  98.5 17.2 %scatter_custom_fusion = bf16[1456,2560]{1,0:T(8,128)(2,1)} fusion(s32[1152]{0:T(1024)S(1)} %fusion.48, bf16[1152,2560]{1,0:T(8,128)(2,1)} %reshape.347, bf16[]{:T(256)} %constant.73.clone.1), kind=kCustom, calls=%fused_computation.18 | custom fusion | bytes 7455232 | tf_op jit(solution)/shard_map/scatter | solution.py:76
  115.7 6.3 %reshape.314 = bf16[2,8,91,2560]{3,2,1,0:T(8,128)(2,1)} reshape(bf16[1456,2560]{1,0:T(8,128)(2,1)} %scatter_custom_fusion) | data formatting | bytes 14909440 | tf_op jit(solution)/shard_map/reshape | solution.py:77
  121.9 27.5 %copy.66 = bf16[2,8,91,2560]{3,0,2,1:T(2,128)(2,1)S(1)} copy(bf16[2,8,91,2560]{3,2,1,0:T(8,128)(2,1)} %reshape.314) | data formatting | bytes 14909440 | tf_op jit(solution)/shard_map/reshape | solution.py:77
  149.4 87.5 %all_to_all.10 = bf16[2,8,91,2560]{3,0,2,1:T(2,128)(2,1)S(1)} all-to-all(bf16[2,8,91,2560]{3,0,2,1:T(2,128)(2,1)S(1)} %copy.66), channel_id=1, replica_groups=mesh['req'=8,'tp'=4] {'req'}, dimensions={1} | all-to-all | bytes 14909440 | tf_op jit(solution)/shard_map/all_to_all | solution.py:139
  236.9 9.0 %fusion = f32[2,728,2,384]{3,1,2,0:T(8,128)S(1)} fusion(bf16[2,2560,2,384]{3,2,1,0:T(2,128)(2,1)} %param.30, bf16[2,728,2560,1]{2,0,1,3:T(2,128)(2,1)S(1)} %bitcast.150), kind=kOutput, calls=%fused_computation.4 | convolution fusion | flops 5725224960 | bytes 19791872 | tf_op jit(solution)/shard_map/emd,edcf->emcf/dot_general | solution.py:141
  245.9 6.1 %convolution_convert_fusion = bf16[2,728,2560]{2,1,0:T(8,128)(2,1)} fusion(bf16[2,384,2560]{2,1,0:T(8,128)(2,1)S(1)} %copy-done.9, f32[2,728,2,384]{3,1,2,0:T(8,128)S(1)} %fusion), kind=kOutput, calls=%fused_computation.7 | convolution fusion | flops 2869694464 | bytes 15859712 | tf_op jit(solution)/shard_map/emf,efd->emd/dot_general | solution.py:146
  252.0 20.1 %copy.85 = bf16[2,728,2560]{1,0,2:T(2,128)(2,1)} copy(bf16[2,728,2560]{2,1,0:T(8,128)(2,1)} %convolution_convert_fusion) | data formatting | bytes 14909440
  272.1 18.3 %reshape.365 = bf16[2560,1456]{1,0:T(8,128)(2,1)} reshape(bf16[2560,2,728]{2,1,0:T(2,128)(2,1)} %bitcast.148) | data formatting | bytes 14909440
  290.5 0.3 reduce-scatter.7.cloned.1.call-start
  290.8 3.2 fusion.4
  294.0 0.7 convolution_convert_fusion.1
  294.7 1.4 copy.83
  296.1 128.2 %reduce-scatter.9.cloned.1.call-done = bf16[640,1456]{1,0:T(8,128)(2,1)} async-done(((bf16[2560,1456]{1,0:T(8,128)(2,1)}), bf16[640,1456]{1,0:T(8,128)(2,1)}) %reduce-scatter.9.cloned.1.call-update) | async-done | bytes 1863696
  424.4 5.2 %reshape.366 = bf16[640,2,728]{2,1,0:T(2,128)(2,1)S(1)} reshape(bf16[640,1456]{1,0:T(8,128)(2,1)} %reduce-scatter.9.cloned.1.call-done) | data formatting | bytes 3727360
  429.5 5.0 %copy.82 = bf16[2,728,640]{2,0,1:T(2,128)(2,1)} copy(bf16[2,728,640]{1,0,2:T(2,128)(2,1)S(1)} %bitcast.149) | data formatting | bytes 3727360 | tf_op jit(solution)/shard_map/reshape | solution.py:151
  434.5 3.8 all-to-all-start.1
  438.3 1.5 convert_element_type.77
  439.8 1.8 fusion.14
  441.7 0.8 copy.72
  442.4 16.1 %reduce-scatter.7.cloned.1.call-done = bf16[640,192]{1,0:T(8,128)(2,1)} async-done(((bf16[2560,192]{1,0:T(8,128)(2,1)}), bf16[640,192]{1,0:T(8,128)(2,1)}) %reduce-scatter.7.cloned.1.call-update) | async-done | bytes 245776
  458.5 1.1 copy.84
  459.7 2.7 all-to-all-done.1
  462.4 1.5 copy.71
  463.9 1.8 reshape.317
  465.8 4.8 gather_fusion.2
  470.6 4.0 reshape.318
  474.5 3.4 multiply_reduce_fusion
  477.9 1.8 add_convert_fusion.1
  (42 shorter events, 0.4 us)
Async XLA Ops:
  6.5 20.8 %copy-start = (bf16[640,2560]{1,0:T(8,128)(2,1)S(1)}, bf16[640,2560]{1,0:T(8,128)(2,1)}, u32[]{:S(2)}) copy-start(bf16[640,2560]{1,0:T(8,128)(2,1)} %param.26) | copy-start | bytes 9830404
  6.5 75.4 %all-reduce.2.cloned.1.call-start = ((), (), s32[]{:S(2)}) async-start(), calls=%async_computation.4 | async-start | bytes 1966080 | tf_op jit(solution)/shard_map/psum | solution.py:131
  11.9 5.6 %copy-start.6 = (bf16[192,128]{1,0:T(8,128)(2,1)S(1)}, bf16[192,128]{1,0:T(8,128)(2,1)}, u32[]{:S(2)}) copy-start(bf16[192,128]{1,0:T(8,128)(2,1)} %param.18) | copy-start | bytes 147460
  15.4 2.2 copy-start.3
  17.6 1.9 copy-start.2
  18.0 2.4 copy-start.4
  23.4 3.5 copy-start.5
  23.4 3.5 copy-start.12
  26.9 2.6 copy-start.7
  29.3 54.7 %copy-start.8 = (f32[2560]{0:T(1024)S(1)}, f32[2560]{0:T(1024)}, u32[]{:S(2)}) copy-start(f32[2560]{0:T(1024)} %param.27) | copy-start | bytes 30724
  29.3 395.0 %reduce-scatter.9.cloned.1.call-start = ((), (), s32[]{:S(2)}) async-start(), calls=%async_computation.6 | async-start | bytes 9830400
  236.9 9.0 %copy-start.9 = (bf16[2,384,2560]{2,1,0:T(8,128)(2,1)S(1)}, bf16[2,384,2560]{2,1,0:T(8,128)(2,1)}, u32[]{:S(2)}) copy-start(bf16[2,384,2560]{2,1,0:T(8,128)(2,1)} %param.31) | copy-start | bytes 11796484
  290.5 168.1 %reduce-scatter.7.cloned.1.call-start = ((), (), s32[]{:S(2)}) async-start(), calls=%async_computation.5 | async-start | bytes 1638400
  290.8 3.2 copy-start.10
  434.5 5.3 %copy-start.11 = (f32[2560,16]{0,1:T(8,128)S(1)}, f32[2560,16]{0,1:T(8,128)}, u32[]{:S(2)}) copy-start(f32[2560,16]{0,1:T(8,128)} %param.28) | copy-start | bytes 491524
  434.5 27.9 %all-to-all-start.1 = ((bf16[2,8,91,640]{3,0,2,1:T(2,128)(2,1)}), bf16[2,8,91,640]{3,0,2,1:T(2,128)(2,1)S(1)}, u32[]{:S(2)}, u32[]{:S(2)}) async-start(bf16[2,8,91,640]{3,0,2,1:T(2,128)(2,1)} %bitcast.151), calls=%async_computation.1 | async-start | bytes 3727360 | tf_op jit(solution)/shard_map/all_to_all | solution.py:152
  470.6 9.1 %copy-start.1 = (bf16[640,2560]{1,0:T(8,128)(2,1)S(1)}, bf16[640,2560]{1,0:T(8,128)(2,1)}, u32[]{:S(2)}) copy-start(bf16[640,2560]{1,0:T(8,128)(2,1)} %param.26) | copy-start | bytes 9830404
Sparse Core Ops, SparseCore 0:
  29.4 52.4 all-reduce.1
  290.6 133.7 reduce-scatter.8
  426.8 31.7 reduce-scatter.6
where the time goes:
time: 488 us; the launch traced here: 486 us
  waiting for transfers between devices  194 us (40%)
  local copies, waits for them, and re-layouts  140 us (29%)
  blocking collectives  87.5 us (18%)
  matrix products  31.1 us (6%)
  other arithmetic  16.7 us (3%)
  between operations  13.5 us (3%)
    unnamed x5, waiting for transfers between devices  144 us
    all_to_all x1, blocking collectives, shards(): lax.all_to_all(outbox, 'req', split_axis=1, concat_axis=1, tiled=True)  87.5 us
    unnamed x32, local copies, waits for them, and re-layouts  47.7 us
    psum x1, waiting for transfers between devices, shards(): lax.psum(attn_terms.astype(jnp.bfloat16), 'tp').astype(jnp.float32)  46.5 us
    reshape x2, local copies, waits for them, and re-layouts, fill_outbox(): return outbox.reshape(lead_shape + (row_values.shape[1],))  33.8 us
    scatter x1, local copies, waits for them, and re-layouts, fill_outbox(): outbox = outbox.at[slot_index].set(repeated)  17.2 us
    reshape x1, local copies, waits for them, and re-layouts, fill_outbox(): repeated = jnp.repeat(row_values, top_count, axis=0)  10.2 us
  transfers between devices with their start and end apart: 4, of which 4 were waited for; matrix products, arithmetic and copies ran while one was open for 5% of the time, Pallas kernels for 0%

commit v1 on v0

--- a/solution.py
+++ b/solution.py
@@ -128,7 +128,11 @@
     capacity = max(10 * requests, row_count * top_count * 5 // (4 * expert_count) + 1)
     slot_index = place_rows(routes, experts_local, groups, capacity)
     lead_shape = (experts_local, groups, capacity)
-    attn_out = lax.psum(attn_terms.astype(jnp.bfloat16), "tp").astype(jnp.float32)
+    attn_out = (
+        lax.all_gather(attn_terms.astype(jnp.bfloat16), axis_name="tp")
+        .sum(axis=0)
+        .astype(jnp.float32)
+    )
     hidden = rounded(residual.astype(jnp.float32) + attn_out)
     rstd = lax.rsqrt(jnp.mean(hidden * hidden, axis=1, keepdims=True) + EPSILON)
     normed = hidden * rstd * norm_gain

time: 488 us -> 515 us (1.055)
  waiting for transfers between devices: 194 us -> 219 us
    all_gather x0 -> x1, waiting for transfers between devices: none -> 73.1 us  [shards(): lax.all_gather(attn_terms.astype(jnp.bfloat16), axis_name='tp').sum(axis=0)]
    psum x1 -> x0, waiting for transfers between devices: 46.5 us -> none  [shards(): lax.psum(attn_terms.astype(jnp.bfloat16), 'tp').astype(jnp.float32)]
    unnamed x32 -> x34, local copies, waits for them, and re-layouts: 47.7 us -> 47.8 us
where the time goes in v1:
time: 515 us; the launch traced here: 514 us
  waiting for transfers between devices  219 us (43%)
  local copies, waits for them, and re-layouts  140 us (27%)
  blocking collectives  87.5 us (17%)
  matrix products  31.1 us (6%)
  other arithmetic  18.4 us (4%)
  between operations  13.5 us (3%)
    unnamed x5, waiting for transfers between devices  143 us
    all_to_all x1, blocking collectives, shards(): lax.all_to_all(outbox, 'req', split_axis=1, concat_axis=1, tiled=True)  87.5 us
    all_gather x1, waiting for transfers between devices, shards(): lax.all_gather(attn_terms.astype(jnp.bfloat16), axis_name='tp').sum(axis=0)  73.1 us
    unnamed x34, local copies, waits for them, and re-layouts  47.8 us
    reshape x2, local copies, waits for them, and re-layouts, fill_outbox(): return outbox.reshape(lead_shape + (row_values.shape[1],))  33.8 us
    scatter x1, local copies, waits for them, and re-layouts, fill_outbox(): outbox = outbox.at[slot_index].set(repeated)  17.2 us
  transfers between devices with their start and end apart: 4, of which 4 were waited for; matrix products, arithmetic and copies ran while one was open for 5% of the time, Pallas kernels for 0%

profile of v1, /device:TPU:0, one launch (start us, length us, event | category | flops | bytes accessed | tf_op | source)
XLA Modules:
  0.0 513.8 jit_solution(17823615058921914805)
XLA Ops:
  6.6 0.8 compare_select_fusion.4
  7.5 0.8 iota_compare_fusion.5
  8.3 2.0 reshape.306
  10.2 1.0 convolution_minimum_fusion.5
  11.2 0.2 convolution_minimum_fusion.4
  11.5 0.2 convolution_minimum_fusion.3
  11.7 0.2 convolution_minimum_fusion.2
  11.9 0.2 convolution_minimum_fusion.1
  12.2 0.2 fusion.22
  12.4 0.1 copy.58
  12.5 2.9 gather_fusion.1
  15.4 2.1 bitcast_reduce_fusion
  17.6 0.4 fusion.55
  18.0 1.4 copy-done.2
  19.4 1.0 fusion.8
  20.4 0.1 fusion.28
  20.5 2.9 gather_fusion
  23.4 3.5 fusion.11
  26.9 0.3 fusion.21
  27.2 0.1 copy.61
  27.4 1.9 convolution_convert_fusion.2
  29.3 0.2 reduce-scatter.9.cloned.1.call-start
  29.5 0.1 copy.63
  29.7 0.1 eq.80
  29.8 0.1 eq.76
  29.9 0.1 reshape.311
  30.1 4.6 reduce-window.6
  34.7 0.4 slice_reduce_fusion
  35.1 0.2 reduce-window.9
  35.5 73.1 %all-gather.3.cloned.1.call-done = bf16[768,2560]{1,0:T(8,128)(2,1)} async-done(((bf16[192,2560]{1,0:T(8,128)(2,1)}), bf16[768,2560]{1,0:T(8,128)(2,1)}) %all-gather.3.cloned.1.call-update) | async-done | bytes 3932176 | tf_op jit(solution)/shard_map/all_gather | solution.py:132
  108.6 3.2 reduce_sum.79
  111.8 0.2 add_convert_fusion
  112.0 0.3 multiply_reduce_fusion.1
  112.3 0.3 fusion.15
  112.6 4.0 broadcast_in_dim.72
  116.6 10.2 %reshape.347 = bf16[1152,2560]{1,0:T(8,128)(2,1)} reshape(bf16[192,6,2560]{2,1,0:T(8,128)(2,1)} %broadcast_in_dim.72) | data formatting | bytes 11796480 | tf_op jit(solution)/shard_map/reshape | solution.py:72
  126.8 17.2 %scatter_custom_fusion = bf16[1456,2560]{1,0:T(8,128)(2,1)} fusion(s32[1152]{0:T(1024)S(1)} %fusion.48, bf16[1152,2560]{1,0:T(8,128)(2,1)} %reshape.347, bf16[]{:T(256)} %constant.69.clone.1), kind=kCustom, calls=%fused_computation.18 | custom fusion | bytes 7455232 | tf_op jit(solution)/shard_map/scatter | solution.py:76
  144.0 6.3 %reshape.314 = bf16[2,8,91,2560]{3,2,1,0:T(8,128)(2,1)} reshape(bf16[1456,2560]{1,0:T(8,128)(2,1)} %scatter_custom_fusion) | data formatting | bytes 14909440 | tf_op jit(solution)/shard_map/reshape | solution.py:77
  150.2 27.5 %copy.66 = bf16[2,8,91,2560]{3,0,2,1:T(2,128)(2,1)S(1)} copy(bf16[2,8,91,2560]{3,2,1,0:T(8,128)(2,1)} %reshape.314) | data formatting | bytes 14909440 | tf_op jit(solution)/shard_map/reshape | solution.py:77
  177.7 87.5 %all_to_all.10 = bf16[2,8,91,2560]{3,0,2,1:T(2,128)(2,1)S(1)} all-to-all(bf16[2,8,91,2560]{3,0,2,1:T(2,128)(2,1)S(1)} %copy.66), channel_id=1, replica_groups=mesh['req'=8,'tp'=4] {'req'}, dimensions={1} | all-to-all | bytes 14909440 | tf_op jit(solution)/shard_map/all_to_all | solution.py:143
  265.2 9.0 %fusion = f32[2,728,2,384]{3,1,2,0:T(8,128)S(1)} fusion(bf16[2,2560,2,384]{3,2,1,0:T(2,128)(2,1)} %param.30, bf16[2,728,2560,1]{2,0,1,3:T(2,128)(2,1)S(1)} %bitcast.151), kind=kOutput, calls=%fused_computation.4 | convolution fusion | flops 5725224960 | bytes 19791872 | tf_op jit(solution)/shard_map/emd,edcf->emcf/dot_general | solution.py:145
  274.3 6.2 %convolution_convert_fusion = bf16[2,728,2560]{2,1,0:T(8,128)(2,1)} fusion(bf16[2,384,2560]{2,1,0:T(8,128)(2,1)S(1)} %copy-done.10, f32[2,728,2,384]{3,1,2,0:T(8,128)S(1)} %fusion), kind=kOutput, calls=%fused_computation.7 | convolution fusion | flops 2869694464 | bytes 15859712 | tf_op jit(solution)/shard_map/emf,efd->emd/dot_general | solution.py:150
  280.4 20.1 %copy.85 = bf16[2,728,2560]{1,0,2:T(2,128)(2,1)} copy(bf16[2,728,2560]{2,1,0:T(8,128)(2,1)} %convolution_convert_fusion) | data formatting | bytes 14909440
  300.5 18.3 %reshape.366 = bf16[2560,1456]{1,0:T(8,128)(2,1)} reshape(bf16[2560,2,728]{2,1,0:T(2,128)(2,1)} %bitcast.149) | data formatting | bytes 14909440
  318.8 0.3 reduce-scatter.7.cloned.1.call-start
  319.2 3.2 fusion.4
  322.4 0.7 convolution_convert_fusion.1
  323.1 1.4 copy.83
  324.5 127.4 %reduce-scatter.9.cloned.1.call-done = bf16[640,1456]{1,0:T(8,128)(2,1)} async-done(((bf16[2560,1456]{1,0:T(8,128)(2,1)}), bf16[640,1456]{1,0:T(8,128)(2,1)}) %reduce-scatter.9.cloned.1.call-update) | async-done | bytes 1863696
  451.9 5.2 %reshape.367 = bf16[640,2,728]{2,1,0:T(2,128)(2,1)S(1)} reshape(bf16[640,1456]{1,0:T(8,128)(2,1)} %reduce-scatter.9.cloned.1.call-done) | data formatting | bytes 3727360
  457.1 5.0 copy.82
  462.1 3.8 all-to-all-start.1
  465.9 1.5 convert_element_type.79
  467.4 1.8 fusion.14
  469.2 0.8 copy.72
  470.0 16.0 %reduce-scatter.7.cloned.1.call-done = bf16[640,192]{1,0:T(8,128)(2,1)} async-done(((bf16[2560,192]{1,0:T(8,128)(2,1)}), bf16[640,192]{1,0:T(8,128)(2,1)}) %reduce-scatter.7.cloned.1.call-update) | async-done | bytes 245776
  486.0 1.1 copy.84
  487.2 2.8 all-to-all-done.1
  490.0 1.5 copy.71
  491.5 1.8 reshape.317
  493.3 4.8 gather_fusion.2
  498.1 4.0 reshape.318
  502.1 3.4 multiply_reduce_fusion
  505.5 1.8 add_convert_fusion.1
  (45 shorter events, 0.5 us)
Async XLA Ops:
  6.5 20.8 %copy-start = (bf16[640,2560]{1,0:T(8,128)(2,1)S(1)}, bf16[640,2560]{1,0:T(8,128)(2,1)}, u32[]{:S(2)}) copy-start(bf16[640,2560]{1,0:T(8,128)(2,1)} %param.26) | copy-start | bytes 9830404
  6.5 102.0 %all-gather.3.cloned.1.call-start = ((), (), s32[]{:S(2)}) async-start(), calls=%async_computation.4 | async-start | bytes 4915200 | tf_op jit(solution)/shard_map/all_gather | solution.py:132
  11.9 5.6 %copy-start.7 = (bf16[192,128]{1,0:T(8,128)(2,1)S(1)}, bf16[192,128]{1,0:T(8,128)(2,1)}, u32[]{:S(2)}) copy-start(bf16[192,128]{1,0:T(8,128)(2,1)} %param.18) | copy-start | bytes 147460
  15.4 2.2 copy-start.3
  17.6 1.9 copy-start.2
  18.0 2.4 copy-start.4
  23.4 3.5 copy-start.5
  23.4 3.5 copy-start.13
  26.9 2.6 copy-start.8
  29.3 82.5 %copy-start.6 = (bf16[192,2560]{1,0:T(8,128)(2,1)S(1)}, bf16[192,2560]{1,0:T(8,128)(2,1)}, u32[]{:S(2)}) copy-start(bf16[192,2560]{1,0:T(8,128)(2,1)} %param.25) | copy-start | bytes 2949124
  29.3 422.6 %reduce-scatter.9.cloned.1.call-start = ((), (), s32[]{:S(2)}) async-start(), calls=%async_computation.6 | async-start | bytes 9830400
  108.6 3.7 copy-start.9
  265.2 9.0 %copy-start.10 = (bf16[2,384,2560]{2,1,0:T(8,128)(2,1)S(1)}, bf16[2,384,2560]{2,1,0:T(8,128)(2,1)}, u32[]{:S(2)}) copy-start(bf16[2,384,2560]{2,1,0:T(8,128)(2,1)} %param.31) | copy-start | bytes 11796484
  318.8 167.2 %reduce-scatter.7.cloned.1.call-start = ((), (), s32[]{:S(2)}) async-start(), calls=%async_computation.5 | async-start | bytes 1638400
  319.1 3.2 copy-start.11
  462.1 5.3 %copy-start.12 = (f32[2560,16]{0,1:T(8,128)S(1)}, f32[2560,16]{0,1:T(8,128)}, u32[]{:S(2)}) copy-start(f32[2560,16]{0,1:T(8,128)} %param.28) | copy-start | bytes 491524
  462.1 27.9 %all-to-all-start.1 = ((bf16[2,8,91,640]{3,0,2,1:T(2,128)(2,1)}), bf16[2,8,91,640]{3,0,2,1:T(2,128)(2,1)S(1)}, u32[]{:S(2)}, u32[]{:S(2)}) async-start(bf16[2,8,91,640]{3,0,2,1:T(2,128)(2,1)} %bitcast.152), calls=%async_computation.1 | async-start | bytes 3727360 | tf_op jit(solution)/shard_map/all_to_all | solution.py:156
  498.1 9.1 %copy-start.1 = (bf16[640,2560]{1,0:T(8,128)(2,1)S(1)}, bf16[640,2560]{1,0:T(8,128)(2,1)}, u32[]{:S(2)}) copy-start(bf16[640,2560]{1,0:T(8,128)(2,1)} %param.26) | copy-start | bytes 9830404
Sparse Core Ops, SparseCore 0:
  29.4 79.1 all-gather.2
  319.0 132.9 reduce-scatter.8
  454.2 31.7 reduce-scatter.6
